TPU v7x, 32 devices: a whole 2x2x4 slice. The times are simulated.
32 devices in a mesh: col: 8 (over y, x, core), row: 4 (over z).
Axes of the slice: x: 2, y: 2, z: 4, core: 2. Of those that a mesh axis runs over, the one named last changes fastest.
Arguments:
- p_blocks: bfloat16 [4, 72, 4096], P('row', 'col'), may hold values from -0.5390625 to 0.5390625
- p_slots: int32 [4, 72], P('row', 'col'), may hold values from 0 to 18, as said below
- out_slots: int32 [4, 104], P('row', 'col'), may hold values from 0 to 18, as said below
Outputs:
- purified: float32 [4, 104, 4096], P('row', 'col')
Inputs may be any that keep to these rules, and one draw needn't show every extreme that they name: `p_slots`: on each device the used slots (entries below 18) come first and name distinct positions; the remaining slots hold 18. Each device uses between half of its 9 slots (rounded up) and all of them, and some device uses all. `out_slots`: on each device the used slots (entries below 18) come first and name distinct positions; the remaining slots hold 18. Each device uses between half of its 13 slots (rounded up) and all of them, and some device uses all.
All inputs are finite; a program needn't handle non-finite values.
Results may differ from a plain program's by a relative error of at most 0.0003.
Values may be sent and summed in bfloat16 or wider, within the bound.
No kernel may reach another device: no remote copies, remote signals or barrier semaphores. Data moves between devices by JAX's collectives and lax.ppermute only.
A program may use at most 192 MiB of HBM per device.

v0:
```python
import jax
import jax.numpy as jnp
from jax import lax
from jax.sharding import PartitionSpec as P

BLK = 64
COLS_DEV = 3


def on_device(p_blocks, p_slots, out_slots):
    n_row = lax.axis_size("row")
    n_col = lax.axis_size("col")
    capacity = p_slots.shape[1]
    block_edge = BLK
    area = block_edge * block_edge
    rows_dev = COLS_DEV * n_col // n_row
    cells = rows_dev * COLS_DEV
    blocks_total = rows_dev * n_row
    width = COLS_DEV * block_edge
    height = rows_dev * block_edge
    own_ids = p_slots[0]
    id_row = jnp.zeros((1, area), jnp.bfloat16)
    id_row = id_row.at[0, :capacity].set(own_ids.astype(jnp.bfloat16))
    payload = jnp.concatenate([p_blocks[0], id_row], axis=0)
    down = lax.all_gather(payload, "row", axis=0, tiled=False)
    down_ids = down[:, capacity, :capacity].astype(jnp.int32)
    down_row = jnp.arange(n_row, dtype=jnp.int32)[:, None] * rows_dev + down_ids // COLS_DEV
    down_index = jnp.where(
        down_ids < cells, down_row * COLS_DEV + down_ids % COLS_DEV, blocks_total * COLS_DEV
    )
    column_grid = jnp.zeros((blocks_total * COLS_DEV, area), jnp.bfloat16)
    column_grid = column_grid.at[down_index.reshape(-1)].set(
        down[:, :capacity].reshape(n_row * capacity, area), mode="drop"
    )
    column_panel = (
        column_grid.reshape(blocks_total, COLS_DEV, block_edge, block_edge)
        .transpose(0, 2, 1, 3)
        .reshape(blocks_total * block_edge, width)
    )
    across = lax.all_gather(payload, "col", axis=0, tiled=False)
    across_ids = across[:, capacity, :capacity].astype(jnp.int32)
    across_col = jnp.arange(n_col, dtype=jnp.int32)[:, None] * COLS_DEV + across_ids % COLS_DEV
    across_index = jnp.where(
        across_ids < cells,
        across_ids // COLS_DEV * blocks_total + across_col,
        rows_dev * blocks_total,
    )
    row_grid = jnp.zeros((rows_dev * blocks_total, area), jnp.bfloat16)
    row_grid = row_grid.at[across_index.reshape(-1)].set(
        across[:, :capacity].reshape(n_col * capacity, area), mode="drop"
    )
    row_panel = (
        row_grid.reshape(rows_dev, blocks_total, block_edge, block_edge)
        .transpose(0, 2, 1, 3)
        .reshape(height, blocks_total * block_edge)
    )
    square = jnp.dot(row_panel, column_panel, preferred_element_type=jnp.float32)
    square_panel = lax.all_gather(square, "row", axis=0, tiled=True)
    cube = jnp.dot(
        row_panel.astype(jnp.float32),
        square_panel,
        precision=lax.Precision.HIGHEST,
        preferred_element_type=jnp.float32,
    )
    combined = 3.0 * square - 2.0 * cube
    new_grid = combined.reshape(rows_dev, block_edge, COLS_DEV, block_edge).transpose(0, 2, 1, 3)
    new_grid = new_grid.reshape(cells, area)
    out_ids = out_slots[0]
    picked = new_grid[jnp.minimum(out_ids, cells - 1)]
    picked = jnp.where((out_ids < cells)[:, None], picked, jnp.zeros_like(picked))
    return picked[None]


def solution(mesh):
    in_specs = (P("row", "col", None), P("row", "col"), P("row", "col"))
    out_specs = P("row", "col", None)
    return jax.shard_map(
        on_device, mesh=mesh, in_specs=in_specs, out_specs=out_specs, check_vma=False
    )
```

profile of v0, /device:TPU:0, one launch (start us, length us, event | category | flops | bytes accessed | tf_op | source)
XLA Modules:
  0.0 100.4 jit_solution(6214441134641464494)
XLA Ops:
  6.5 0.0 all-gather.6.cloned.1.call-start
  6.5 0.6 compare_reduce_fusion.4
  7.2 1.3 %broadcast_select_fusion = bf16[1,9]{1,0:T(2,128)(2,1)S(1)} fusion(pred[]{:T(512)} %compare_reduce_fusion.4, s32[1,9]{1,0:T(1,128)} %param.6), kind=kLoop, calls=%fused_computation.34 | loop fusion | flops 18 | bytes 55 | tf_op jit(solution)/shard_map/select.3
  8.5 0.9 fusion.7
  9.4 12.4 %all-gather.2 = bf16[8,10,4096]{2,1,0:T(8,128)(2,1)S(1)} all-gather(bf16[1,10,4096]{2,1,0:T(8,128)(2,1)S(1)} %fusion.7), channel_id=2, replica_groups=mesh['col'=8,'row'=4] {'col'}, dimensions={0}, use_global_device_ids=true | all-gather | bytes 737280 | tf_op jit(solution)/shard_map/all_gather | solution.py:40
  21.9 16.3 %all-gather.3 = bf16[4,10,4096]{2,1,0:T(8,128)(2,1)S(1)} all-gather(bf16[1,10,4096]{2,1,0:T(8,128)(2,1)S(1)} %fusion.7), channel_id=3, replica_groups=mesh['col'=8,'row'=4] {'row'}, dimensions={0}, use_global_device_ids=true | all-gather | bytes 409600 | tf_op jit(solution)/shard_map/all_gather | solution.py:25
  38.3 0.0 copy-start
  38.3 0.8 copy-done
  39.1 0.5 compare_reduce_fusion.2
  39.6 0.1 div.35
  39.7 0.1 rem.56
  39.8 0.1 lt.92
  39.9 0.1 ne.104
  40.0 0.1 add.140
  40.0 0.1 add.141
  40.1 0.3 reshape.316
  40.4 1.8 %scatter_custom_fusion = bf16[144,4096]{1,0:T(8,128)(2,1)S(1)} fusion(s32[72]{0:T(128)S(1)} %fusion.12, bf16[72,4096]{1,0:T(8,128)(2,1)S(1)} %reshape.316, bf16[]{:T(256)} %constant.75.clone.1), kind=kCustom, calls=%fused_computation.5 | custom fusion | bytes 1179650 | tf_op jit(solution)/shard_map/scatter | solution.py:49
  42.2 2.6 %reshape.297 = bf16[6,24,64,64]{3,2,1,0:T(8,128)(2,1)S(1)} reshape(bf16[144,4096]{1,0:T(8,128)(2,1)S(1)} %scatter_custom_fusion) | data formatting | bytes 2359296 | tf_op jit(solution)/shard_map/reshape | solution.py:53
  44.8 2.9 %copy.12 = bf16[6,64,24,64]{3,2,1,0:T(8,128)(2,1)} copy(bf16[6,64,24,64]{3,1,2,0:T(8,128)(2,1)S(1)} %bitcast.34) | data formatting | bytes 2359296 | tf_op jit(solution)/shard_map/transpose | solution.py:54
  47.7 0.0 copy-start.2
  47.7 0.0 copy-start.1
  47.7 3.5 %reshape.298 = bf16[384,1536]{1,0:T(8,128)(2,1)S(1)} reshape(bf16[6,64,24,64]{3,2,1,0:T(8,128)(2,1)} %copy.12) | data formatting | bytes 2359296 | tf_op jit(solution)/shard_map/reshape | solution.py:55
  51.3 0.1 div.37
  51.3 0.1 rem.60
  51.4 0.0 copy-done.2
  51.4 0.1 lt.97
  51.5 0.1 ne.109
  51.6 0.1 add.146
  51.7 0.1 add.147
  51.8 0.0 copy-done.1
  51.8 0.1 reshape.324
  51.9 1.2 %scatter_custom_fusion.1 = bf16[72,4096]{1,0:T(8,128)(2,1)S(1)} fusion(s32[36]{0:T(128)S(1)} %fusion.13, bf16[36,4096]{1,0:T(8,128)(2,1)S(1)} %reshape.324, bf16[]{:T(256)} %constant.75.clone.1), kind=kCustom, calls=%fused_computation.7 | custom fusion | bytes 589826 | tf_op jit(solution)/shard_map/scatter | solution.py:32
  53.1 1.3 %reshape.300 = bf16[24,3,64,64]{3,2,1,0:T(8,128)(2,1)S(1)} reshape(bf16[72,4096]{1,0:T(8,128)(2,1)S(1)} %scatter_custom_fusion.1) | data formatting | bytes 1179648 | tf_op jit(solution)/shard_map/reshape | solution.py:36
  54.4 1.3 %copy.13 = bf16[24,64,3,64]{1,0,3,2:T(8,128)(2,1)S(1)} copy(bf16[24,64,3,64]{3,1,2,0:T(8,128)(2,1)S(1)} %bitcast.35) | data formatting | bytes 1179648 | tf_op jit(solution)/shard_map/transpose | solution.py:37
  55.7 0.7 reshape.301
  56.4 0.0 copy-start.3
  56.4 1.3 %fusion.15 = f32[384,192]{0,1:T(8,128)} fusion(bf16[384,1536]{1,0:T(8,128)(2,1)S(1)} %reshape.298, bf16[1536,192]{0,1:T(8,128)(2,1)S(1)} %reshape.301), kind=kOutput, calls=%fused_computation.44 | convolution fusion | flops 226492416 | bytes 2064384 | tf_op jit(solution)/shard_map/dot_general | solution.py:57
  57.7 0.0 all-gather.6.cloned.1.call-update
  57.7 0.0 copy-done.3
  57.8 30.9 %all-gather.6.cloned.1.call-done = f32[1536,192]{0,1:T(8,128)} async-done(((f32[384,192]{0,1:T(8,128)}), f32[1536,192]{0,1:T(8,128)}) %all-gather.6.cloned.1.call-update) | async-done | bytes 1179664 | tf_op jit(solution)/shard_map/all_gather | solution.py:58
  88.7 2.6 %fusion = f32[384,192]{0,1:T(8,128)S(1)} fusion(bf16[384,1536]{1,0:T(8,128)(2,1)S(1)} %reshape.298, f32[1536,192]{0,1:T(8,128)} %all-gather.6.cloned.1.call-done, f32[384,192]{0,1:T(8,128)} %fusion.15), kind=kOutput, calls=%fused_computation.4 | convolution fusion | flops 1359175680 | bytes 2949120 | tf_op jit(solution)/shard_map/dot_general | solution.py:59
  91.3 0.2 reshape.302
  91.4 0.3 copy.14
  91.7 0.2 reshape.303
  91.9 0.6 gather_fusion
  92.5 0.1 bitcast_select_fusion
  92.6 0.9 copy.15
  (10 shorter events, 0.2 us)
Async XLA Ops:
  6.5 82.2 %all-gather.6.cloned.1.call-start = ((), (), s32[]{:S(2)}) async-start(), calls=%async_computation | async-start | bytes 1474560 | tf_op jit(solution)/shard_map/all_gather | solution.py:58
  38.3 0.8 copy-start
  47.7 3.7 %copy-start.2 = (pred[4,9]{1,0:T(4,128)(4,1)S(1)}, pred[4,9]{1,0:T(4,128)(4,1)}, u32[]{:S(2)}) copy-start(pred[4,9]{1,0:T(4,128)(4,1)} %get-tuple-element.22) | copy-start | bytes 112
  47.7 4.0 %copy-start.1 = (bf16[4,10,4096]{2,1,0:T(8,128)(2,1)S(1)}, bf16[4,10,4096]{2,1,0:T(8,128)(2,1)}, u32[]{:S(2)}) copy-start(bf16[4,10,4096]{2,1,0:T(8,128)(2,1)} %copy-done) | copy-start | bytes 983044
  56.4 1.3 %copy-start.3 = (s32[1,13]{1,0:T(1,128)S(1)}, s32[1,13]{1,0:T(1,128)}, u32[]{:S(2)}) copy-start(s32[1,13]{1,0:T(1,128)} %param.7) | copy-start | bytes 160
Sparse Core Ops, SparseCore 0:
  57.9 30.7 all-gather.5
where the time goes:
time: 101 us; the launch traced here: 100 us
  waiting for transfers between devices  30.9 us (31%)
  blocking collectives  28.8 us (29%)
  local copies, waits for them, and re-layouts  19.6 us (19%)
  between operations  13.6 us (13%)
  matrix products  3.83 us (4%)
  other arithmetic  3.67 us (4%)
    all_gather x1, waiting for transfers between devices, on_device(): square_panel = lax.all_gather(square, 'row', axis=0, tiled=True)  30.9 us
    all_gather x1, blocking collectives, on_device(): down = lax.all_gather(payload, 'row', axis=0, tiled=False)  16.3 us
    all_gather x1, blocking collectives, on_device(): across = lax.all_gather(payload, 'col', axis=0, tiled=False)  12.4 us
    reshape x1, local copies, waits for them, and re-layouts, on_device(): row_panel = row_grid.reshape(rows_dev, blocks_total, block_edge, block_ed...  3.5 us
    transpose x1, local copies, waits for them, and re-layouts, on_device(): row_panel = row_grid.reshape(rows_dev, blocks_total, block_edge, block_ed...  2.94 us
    reshape x1, local copies, waits for them, and re-layouts, on_device(): row_grid.reshape(rows_dev, blocks_total, block_edge, block_edge)  2.57 us
    dot_general x1, matrix products, on_device(): jnp.dot(row_panel.astype(jnp.float32), square_panel, precision=lax.Precis...  2.56 us
  transfers between devices with their start and end apart: 1, of which 1 were waited for; matrix products, arithmetic and copies ran while one was open for 0% of the time, Pallas kernels for 0%

commit v1 on v0

--- a/solution.py
+++ b/solution.py
@@ -1,3 +1,4 @@
+import functools
 import jax
 import jax.numpy as jnp
 from jax import lax
@@ -5,6 +6,34 @@
 
 BLK = 64
 COLS_DEV = 3
+
+
+def work_the_lots_all(frame_in, axis_tag):
+    inter = lax.axis_size(axis_tag)
+    x_now = lax.axis_index(axis_tag)
+    kept_arr, mat_out, ready = (inter, x_now, frame_in.shape[0])
+    copies = []
+    for dd, q in enumerate(frame_in.shape):
+        copies.append(q * kept_arr if dd == 0 else q)
+    earlier = lax.dynamic_update_slice_in_dim(
+        jnp.zeros(copies, frame_in.dtype), frame_in, mat_out * ready, axis=0
+    )
+    dev_i = 1
+    while dev_i < kept_arr:
+        cards = []
+        dd = 0
+        while dd < kept_arr:
+            cards.append((dd, (dd + 1) % kept_arr))
+            dd += 1
+        frame_in = lax.ppermute(frame_in, axis_name=axis_tag, perm=cards)
+        earlier = lax.dynamic_update_slice_in_dim(
+            earlier, frame_in, (mat_out - dev_i) % kept_arr * ready, axis=0
+        )
+        dev_i += 1
+    return earlier
+
+
+end_slices = functools.partial(work_the_lots_all, axis_tag="row")
 
 
 def on_device(p_blocks, p_slots, out_slots):
@@ -55,7 +84,7 @@
         .reshape(height, blocks_total * block_edge)
     )
     square = jnp.dot(row_panel, column_panel, preferred_element_type=jnp.float32)
-    square_panel = lax.all_gather(square, "row", axis=0, tiled=True)
+    square_panel = end_slices(square)
     cube = jnp.dot(
         row_panel.astype(jnp.float32),
         square_panel,

time: 101 us -> 82.5 us (0.82)
  between operations: 13.6 us -> 0.27 us
  waiting for transfers between devices: 30.9 us -> 24.7 us
  matrix products: 3.83 us -> 1.78 us
  starting transfers between devices: 0.01 us -> 1.93 us
  local copies, waits for them, and re-layouts: 19.6 us -> 21 us
    all_gather x1 -> x0, waiting for transfers between devices: 30.9 us -> none  [on_device(): square_panel = lax.all_gather(square, 'row', axis=0, tiled=True)]
    ppermute x0 -> x3, waiting for transfers between devices: none -> 24.7 us  [work_the_lots_all(): frame_in = lax.ppermute(frame_in, axis_name=axis_tag, perm=cards)]
    ppermute x0 -> x3, starting transfers between devices: none -> 1.93 us  [work_the_lots_all(): frame_in = lax.ppermute(frame_in, axis_name=axis_tag, perm=cards)]
    dot_general x1, matrix products: 2.56 us -> 1.25 us  [on_device(): jnp.dot(row_panel.astype(jnp.float32), square_panel, precision=lax.Precis...]
  transfers between devices with their start and end apart: 1 -> 3, of which waited for: 1 -> 3; matrix products, arithmetic and copies ran while one was open for 0% -> 0% of each run, Pallas kernels for 0% -> 0%
where the time goes in v1:
time: 82.5 us; the launch traced here: 82.2 us
  blocking collectives  28.8 us (35%)
  waiting for transfers between devices  24.7 us (30%)
  local copies, waits for them, and re-layouts  21 us (25%)
  other arithmetic  3.72 us (5%)
  starting transfers between devices  1.93 us (2%)
  matrix products  1.78 us (2%)
    ppermute x3, waiting for transfers between devices, work_the_lots_all(): frame_in = lax.ppermute(frame_in, axis_name=axis_tag, perm=cards)  24.7 us
    all_gather x1, blocking collectives, on_device(): down = lax.all_gather(payload, 'row', axis=0, tiled=False)  16.3 us
    all_gather x1, blocking collectives, on_device(): across = lax.all_gather(payload, 'col', axis=0, tiled=False)  12.4 us
    reshape x1, local copies, waits for them, and re-layouts, on_device(): row_panel = row_grid.reshape(rows_dev, blocks_total, block_edge, block_ed...  3.5 us
    transpose x1, local copies, waits for them, and re-layouts, on_device(): row_panel = row_grid.reshape(rows_dev, blocks_total, block_edge, block_ed...  2.94 us
    reshape x1, local copies, waits for them, and re-layouts, on_device(): row_grid.reshape(rows_dev, blocks_total, block_edge, block_edge)  2.57 us
    another operation x2, other arithmetic  1.94 us
    ppermute x3, starting transfers between devices, work_the_lots_all(): frame_in = lax.ppermute(frame_in, axis_name=axis_tag, perm=cards)  1.93 us
  transfers between devices with their start and end apart: 3, of which 3 were waited for; matrix products, arithmetic and copies ran while one was open for 0% of the time, Pallas kernels for 0%

profile of v1, /device:TPU:0, one launch (start us, length us, event | category | flops | bytes accessed | tf_op | source)
XLA Modules:
  0.0 82.2 jit_solution(6766210055116308255)
XLA Ops:
  0.0 0.6 compare_reduce_fusion.4
  0.6 1.3 %broadcast_select_fusion = bf16[1,9]{1,0:T(2,128)(2,1)S(1)} fusion(pred[]{:T(512)} %compare_reduce_fusion.4, s32[1,9]{1,0:T(1,128)} %param.6), kind=kLoop, calls=%fused_computation.38 | loop fusion | flops 18 | bytes 55 | tf_op jit(solution)/shard_map/select.9
  1.9 0.9 %fusion.7 = bf16[1,10,4096]{2,1,0:T(8,128)(2,1)S(1)} fusion(bf16[1,9]{1,0:T(2,128)(2,1)S(1)} %broadcast_select_fusion, bf16[9,4096]{1,0:T(8,128)(2,1)} %bitcast.39), kind=kLoop, calls=%fused_computation.13 | loop fusion | flops 245760 | bytes 155666
  2.9 12.4 %all-gather.2 = bf16[8,10,4096]{2,1,0:T(8,128)(2,1)S(1)} all-gather(bf16[1,10,4096]{2,1,0:T(8,128)(2,1)S(1)} %fusion.7), channel_id=2, replica_groups=mesh['col'=8,'row'=4] {'col'}, dimensions={0}, use_global_device_ids=true | all-gather | bytes 737280 | tf_op jit(solution)/shard_map/all_gather | solution.py:69
  15.4 16.3 %all-gather.3 = bf16[4,10,4096]{2,1,0:T(8,128)(2,1)S(1)} all-gather(bf16[1,10,4096]{2,1,0:T(8,128)(2,1)S(1)} %fusion.7), channel_id=3, replica_groups=mesh['col'=8,'row'=4] {'row'}, dimensions={0}, use_global_device_ids=true | all-gather | bytes 409600 | tf_op jit(solution)/shard_map/all_gather | solution.py:54
  31.7 0.6 compare_reduce_fusion.2
  32.3 0.2 copy-done.1
  32.6 0.1 lt.118
  32.7 0.1 add.165
  32.8 0.1 add.166
  32.8 0.1 rem.96
  32.9 0.1 div.35
  33.0 0.1 ne.118
  33.1 0.3 reshape.316
  33.4 1.8 %scatter_custom_fusion = bf16[144,4096]{1,0:T(8,128)(2,1)S(1)} fusion(s32[72]{0:T(128)S(1)} %fusion.12, bf16[72,4096]{1,0:T(8,128)(2,1)S(1)} %reshape.316, bf16[]{:T(256)} %constant.105.clone.1), kind=kCustom, calls=%fused_computation.5 | custom fusion | bytes 1179650 | tf_op jit(solution)/shard_map/scatter | solution.py:78
  35.2 2.6 %reshape.297 = bf16[6,24,64,64]{3,2,1,0:T(8,128)(2,1)S(1)} reshape(bf16[144,4096]{1,0:T(8,128)(2,1)S(1)} %scatter_custom_fusion) | data formatting | bytes 2359296 | tf_op jit(solution)/shard_map/reshape | solution.py:82
  37.8 2.9 %copy.12 = bf16[6,64,24,64]{3,2,1,0:T(8,128)(2,1)} copy(bf16[6,64,24,64]{3,1,2,0:T(8,128)(2,1)S(1)} %bitcast.34) | data formatting | bytes 2359296 | tf_op jit(solution)/shard_map/transpose | solution.py:83
  40.7 3.5 %reshape.298 = bf16[384,1536]{1,0:T(8,128)(2,1)S(1)} reshape(bf16[6,64,24,64]{3,2,1,0:T(8,128)(2,1)} %copy.12) | data formatting | bytes 2359296 | tf_op jit(solution)/shard_map/reshape | solution.py:84
  44.2 0.0 copy-done.3
  44.2 0.1 lt.123
  44.3 0.1 rem.100
  44.4 0.1 add.171
  44.5 0.1 add.172
  44.6 0.1 div.37
  44.6 0.1 ne.123
  44.7 0.0 copy-done.2
  44.7 0.1 reshape.324
  44.9 1.2 %scatter_custom_fusion.1 = bf16[72,4096]{1,0:T(8,128)(2,1)S(1)} fusion(s32[36]{0:T(128)S(1)} %fusion.13, bf16[36,4096]{1,0:T(8,128)(2,1)S(1)} %reshape.324, bf16[]{:T(256)} %constant.105.clone.1), kind=kCustom, calls=%fused_computation.7 | custom fusion | bytes 589826 | tf_op jit(solution)/shard_map/scatter | solution.py:61
  46.1 1.3 %reshape.300 = bf16[24,3,64,64]{3,2,1,0:T(8,128)(2,1)S(1)} reshape(bf16[72,4096]{1,0:T(8,128)(2,1)S(1)} %scatter_custom_fusion.1) | data formatting | bytes 1179648 | tf_op jit(solution)/shard_map/reshape | solution.py:65
  47.4 1.3 %copy.13 = bf16[24,64,3,64]{1,0,3,2:T(8,128)(2,1)S(1)} copy(bf16[24,64,3,64]{3,1,2,0:T(8,128)(2,1)S(1)} %bitcast.35) | data formatting | bytes 1179648 | tf_op jit(solution)/shard_map/transpose | solution.py:66
  48.7 1.5 %reshape.301 = bf16[1536,192]{0,1:T(8,128)(2,1)} reshape(bf16[24,64,3,64]{1,0,3,2:T(8,128)(2,1)S(1)} %copy.13) | data formatting | bytes 1179648 | tf_op jit(solution)/shard_map/reshape | solution.py:67
  50.2 0.1 broadcast_in_dim.41
  50.3 0.9 %copy-done = bf16[1536,192]{0,1:T(8,128)(2,1)S(1)} copy-done((bf16[1536,192]{0,1:T(8,128)(2,1)S(1)}, bf16[1536,192]{0,1:T(8,128)(2,1)}, u32[]{:S(2)}) %copy-start) | copy-done | bytes 589848
  51.3 0.5 constant_dynamic-update-slice_fusion.3
  51.8 1.9 %collective-permute-start = (f32[384,192]{0,1:T(8,128)S(1)}, f32[384,192]{0,1:T(8,128)S(1)}, u32[]{:S(2)}, u32[]{:S(2)}) collective-permute-start(f32[384,192]{0,1:T(8,128)S(1)} %get-tuple-element.26), channel_id=1, source_target_pairs={{0,1},{1,2},{2,3},{3,0},{4,5},{5,6},{6,7},{7,4},{8,9},{9,10},{10,1... | collective-permute-start | bytes 884744 | tf_op jit(solution)/shard_map/ppermute | solution.py:28
  53.8 7.7 %collective-permute-done = f32[384,192]{0,1:T(8,128)S(1)} collective-permute-done((f32[384,192]{0,1:T(8,128)S(1)}, f32[384,192]{0,1:T(8,128)S(1)}, u32[]{:S(2)}, u32[]{:S(2)}) %collective-permute-start) | collective-permute-done | bytes 294944 | tf_op jit(solution)/shard_map/ppermute | solution.py:28
  61.4 0.0 collective-permute-start.1
  61.4 0.0 copy-done.4
  61.5 8.7 %collective-permute-done.1 = f32[384,192]{0,1:T(8,128)S(1)} collective-permute-done((f32[384,192]{0,1:T(8,128)S(1)}, f32[384,192]{0,1:T(8,128)S(1)}, u32[]{:S(2)}, u32[]{:S(2)}) %collective-permute-start.1) | collective-permute-done | bytes 294944 | tf_op jit(solution)/shard_map/ppermute | solution.py:28
  70.1 0.0 collective-permute-start.2
  70.3 8.4 %collective-permute-done.2 = f32[384,192]{0,1:T(8,128)S(1)} collective-permute-done((f32[384,192]{0,1:T(8,128)S(1)}, f32[384,192]{0,1:T(8,128)S(1)}, u32[]{:S(2)}, u32[]{:S(2)}) %collective-permute-start.2) | collective-permute-done | bytes 294944 | tf_op jit(solution)/shard_map/ppermute | solution.py:28
  78.7 1.2 %fusion = f32[384,192]{0,1:T(8,128)S(1)} fusion(bf16[384,1536]{1,0:T(8,128)(2,1)S(1)} %reshape.298, f32[1536,192]{0,1:T(8,128)S(1)} %constant_dynamic-update-slice_fusion, f32[384,192]{0,1:T(8,128)S(1)} %get-tuple-element.26), kind=kOutput, calls=%fused_computation.4 | convolution fusion | flops 1359175680 | bytes 2949120 | tf_op jit(solution)/shard_map/dot_general | solution.py:88
  79.9 0.2 reshape.302
  80.1 0.3 copy.14
  80.4 0.2 reshape.303
  80.6 0.6 gather_fusion
  81.2 0.1 bitcast_select_fusion
  81.3 0.9 %copy.15 = f32[1,13,4096]{2,0,1:T(1,128)} copy(f32[1,13,4096]{2,1,0:T(8,128)S(1)} %bitcast_select_fusion) | data formatting | bytes 425984 | tf_op jit(solution)/shard_map/jit(_where)/select_n | solution.py:99
  (18 shorter events, 0.3 us)
Async XLA Ops:
  31.7 0.8 copy-start.1
  40.7 3.5 %copy-start.3 = (pred[4,9]{1,0:T(4,128)(4,1)S(1)}, pred[4,9]{1,0:T(4,128)(4,1)}, u32[]{:S(2)}) copy-start(pred[4,9]{1,0:T(4,128)(4,1)} %get-tuple-element.22) | copy-start | bytes 112
  40.7 4.0 %copy-start.2 = (bf16[4,10,4096]{2,1,0:T(8,128)(2,1)S(1)}, bf16[4,10,4096]{2,1,0:T(8,128)(2,1)}, u32[]{:S(2)}) copy-start(bf16[4,10,4096]{2,1,0:T(8,128)(2,1)} %copy-done.1) | copy-start | bytes 983044
  50.2 1.1 %copy-start = (bf16[1536,192]{0,1:T(8,128)(2,1)S(1)}, bf16[1536,192]{0,1:T(8,128)(2,1)}, u32[]{:S(2)}) copy-start(bf16[1536,192]{0,1:T(8,128)(2,1)} %reshape.301) | copy-start | bytes 1769476
  51.3 10.2 %copy-start.4 = (s32[1,13]{1,0:T(1,128)S(1)}, s32[1,13]{1,0:T(1,128)}, u32[]{:S(2)}) copy-start(s32[1,13]{1,0:T(1,128)} %param.7) | copy-start | bytes 160
  51.8 9.6 %collective-permute-start = (f32[384,192]{0,1:T(8,128)S(1)}, f32[384,192]{0,1:T(8,128)S(1)}, u32[]{:S(2)}, u32[]{:S(2)}) collective-permute-start(f32[384,192]{0,1:T(8,128)S(1)} %get-tuple-element.26), channel_id=1, source_target_pairs={{0,1},{1,2},{2,3},{3,0},{4,5},{5,6},{6,7},{7,4},{8,9},{9,10},{10,1... | collective-permute-start | bytes 884744 | tf_op jit(solution)/shard_map/ppermute | solution.py:28
  61.4 8.7 %collective-permute-start.1 = (f32[384,192]{0,1:T(8,128)S(1)}, f32[384,192]{0,1:T(8,128)S(1)}, u32[]{:S(2)}, u32[]{:S(2)}) collective-permute-start(f32[384,192]{0,1:T(8,128)S(1)} %collective-permute-done), channel_id=1, source_target_pairs={{0,1},{1,2},{2,3},{3,0},{4,5},{5,6},{6,7},{7,4},{8,9},{9,10},{10,1... | collective-permute-start | bytes 884744 | tf_op jit(solution)/shard_map/ppermute | solution.py:28
  70.1 8.5 %collective-permute-start.2 = (f32[384,192]{0,1:T(8,128)S(1)}, f32[384,192]{0,1:T(8,128)S(1)}, u32[]{:S(2)}, u32[]{:S(2)}) collective-permute-start(f32[384,192]{0,1:T(8,128)S(1)} %collective-permute-done.1), channel_id=1, source_target_pairs={{0,1},{1,2},{2,3},{3,0},{4,5},{5,6},{6,7},{7,4},{8,9},{9,10},{10,1... | collective-permute-start | bytes 884744 | tf_op jit(solution)/shard_map/ppermute | solution.py:28
